TPU v7x, 32 devices: a whole 2x2x4 slice. The times are simulated.
32 devices in a mesh: groups: 2 (over x), freq: 16 (over z, y, core).
Axes of the slice: x: 2, y: 2, z: 4, core: 2. Of those that a mesh axis runs over, the one named last changes fastest.
Arguments:
- encoder_input: bfloat16 [64, 2048], P(('groups', 'freq')), parts along dimension 0, may hold values from -6 to 6
- desired_responses: bfloat16 [64, 384, 512], P('groups', 'freq'), parts along dimension 0, may hold values from -6 to 6
- sample_index: int32 [64], P('groups'), parts along dimension 0, may hold values from 0 to 31, each once
- encoder_weight: bfloat16 [2048, 512], replicated, may hold values from -0.125 to 0.125
- decoder_weight: bfloat16 [512, 512], replicated, may hold values from -0.25 to 0.25
- frequency_amplitude: bfloat16 [384, 512], P('freq'), may hold values from -4 to 4
- spectral_filter_weight: float32 [2, 256], replicated, may hold values from -4 to 4
- output_weight: bfloat16 [512, 512], replicated, may hold values from -0.25 to 0.25
Outputs:
- grad_enc: float32 [4096, 512], P('groups'), parts along dimension 0
- grad_dec: float32 [1024, 512], P('groups'), parts along dimension 0
- grad_out: float32 [1024, 512], P('groups'), parts along dimension 0
- grad_filter: float32 [4, 256], P('groups'), parts along dimension 0
There are 2 independent parts, one for each index of `groups`. A program takes and returns all parts, laid end to end along the dimension named above; an argument that names none is the same for every part. Nothing has to cross between parts.
Inputs may be any that keep to these rules, and one draw needn't show every extreme that they name: sample_index names each of the 32 samples once.
All inputs are finite; a program needn't handle non-finite values.
Results may differ from a plain program's by a relative error of at most 0.0065.
Values may be sent and summed in bfloat16 or wider, within the bound.
No kernel may reach another device: no remote copies, remote signals or barrier semaphores. Data moves between devices by JAX's collectives and lax.ppermute only.
A program may use at most 128 MiB of HBM per device.

v0:
```python
import math
import jax
import jax.numpy as jnp
from jax import lax
from jax.sharding import PartitionSpec as P


def rotation_tables(antennas):
    indices = jnp.arange(antennas, dtype=jnp.int32)
    products_mod = indices[:, None] * indices[None, :] % antennas
    angle_table = products_mod.astype(jnp.float32) * (2.0 * math.pi / antennas)
    cosine_table = jnp.cos(angle_table) / math.sqrt(antennas)
    sine_table = jnp.sin(angle_table) / math.sqrt(antennas)
    forward_transform = jnp.concatenate(
        [
            jnp.concatenate([cosine_table, -sine_table], 1),
            jnp.concatenate([sine_table, cosine_table], 1),
        ],
        0,
    )
    inverse_transform = jnp.concatenate(
        [
            jnp.concatenate([cosine_table, sine_table], 1),
            jnp.concatenate([-sine_table, cosine_table], 1),
        ],
        0,
    )
    return (forward_transform.astype(jnp.bfloat16), inverse_transform.astype(jnp.bfloat16))


def decode_rows(
    mixed_in,
    wanted_lines,
    output_weight,
    spectral_filter_weight,
    forward_transform,
    inverse_transform,
    loss_scale,
):
    filter_re = spectral_filter_weight[0]
    filter_im = spectral_filter_weight[1]
    spectrum = jnp.dot(mixed_in, forward_transform, preferred_element_type=jnp.float32)
    half_width = spectrum.shape[1] // 2
    spec_re = spectrum[:, :half_width]
    spec_im = spectrum[:, half_width:]
    filtered = jnp.concatenate(
        [spec_re * filter_re - spec_im * filter_im, spec_re * filter_im + spec_im * filter_re], 1
    ).astype(jnp.bfloat16)
    mixed_back = jnp.dot(filtered, inverse_transform, preferred_element_type=jnp.float32)
    hidden = (mixed_in.astype(jnp.float32) + jax.nn.gelu(mixed_back)).astype(jnp.bfloat16)
    rebuilt = hidden.astype(jnp.float32) + jnp.dot(
        hidden, output_weight, preferred_element_type=jnp.float32
    )
    residual = loss_scale * (rebuilt - wanted_lines.astype(jnp.float32))
    residual_half = residual.astype(jnp.bfloat16)
    grad_out = lax.dot_general(
        hidden, residual_half, (((0,), (0,)), ((), ())), preferred_element_type=jnp.float32
    )
    grad_hidden = residual + lax.dot_general(
        residual_half, output_weight, (((1,), (1,)), ((), ())), preferred_element_type=jnp.float32
    )
    grad_mixed = jax.vjp(jax.nn.gelu, mixed_back)[1](grad_hidden)[0].astype(jnp.bfloat16)
    grad_filtered = lax.dot_general(
        grad_mixed, inverse_transform, (((1,), (1,)), ((), ())), preferred_element_type=jnp.float32
    )
    grad_re = grad_filtered[:, :half_width]
    grad_im = grad_filtered[:, half_width:]
    grad_filter = jnp.stack(
        [
            jnp.sum(grad_re * spec_re + grad_im * spec_im, 0),
            jnp.sum(grad_im * spec_re - grad_re * spec_im, 0),
        ]
    )
    grad_spec = jnp.concatenate(
        [grad_re * filter_re + grad_im * filter_im, grad_im * filter_re - grad_re * filter_im], 1
    ).astype(jnp.bfloat16)
    derivative_entering = grad_hidden + lax.dot_general(
        grad_spec, forward_transform, (((1,), (1,)), ((), ())), preferred_element_type=jnp.float32
    )
    return (derivative_entering, grad_out, grad_filter)


def encoder_grads(inputs_rows, codewords, latent_sums, decoder_weight):
    latent_half = latent_sums.astype(jnp.bfloat16)
    grad_dec = lax.dot_general(
        codewords, latent_half, (((0,), (0,)), ((), ())), preferred_element_type=jnp.float32
    )
    grad_codes = lax.dot_general(
        latent_half, decoder_weight, (((1,), (1,)), ((), ())), preferred_element_type=jnp.float32
    )
    grad_pre = (grad_codes * (1.0 - jnp.square(codewords.astype(jnp.float32)))).astype(jnp.bfloat16)
    grad_enc = lax.dot_general(
        inputs_rows, grad_pre, (((0,), (0,)), ((), ())), preferred_element_type=jnp.float32
    )
    return (grad_enc, grad_dec)


def local(
    encoder_input,
    desired_responses,
    sample_index,
    encoder_weight,
    decoder_weight,
    frequency_amplitude,
    spectral_filter_weight,
    output_weight,
):
    samples = sample_index.shape[0]
    sub_dev = desired_responses.shape[1]
    width = desired_responses.shape[2]
    forward_transform, inverse_transform = rotation_tables(width // 2)
    loss_scale = 1.0 / math.sqrt(samples * sub_dev * lax.axis_size("freq"))
    codes_own = jnp.tanh(
        jnp.dot(encoder_input, encoder_weight, preferred_element_type=jnp.float32)
    ).astype(jnp.bfloat16)
    all_codes = lax.all_gather(codes_own, "freq", axis=0, tiled=True)
    inverse_ids = (
        jnp.zeros((samples,), jnp.int32).at[sample_index].set(jnp.arange(samples, dtype=jnp.int32))
    )
    latent = jnp.dot(all_codes[inverse_ids], decoder_weight, preferred_element_type=jnp.float32)
    gain_row_values = frequency_amplitude.astype(jnp.float32)
    mixed_in = (latent[:, None, :] * gain_row_values[None]).astype(jnp.bfloat16).reshape(-1, width)
    wanted_lines = desired_responses.reshape(-1, width)
    derivative_entering, grad_out, grad_filter = decode_rows(
        mixed_in,
        wanted_lines,
        output_weight,
        spectral_filter_weight,
        forward_transform,
        inverse_transform,
        loss_scale,
    )
    derivative_bottleneck = jnp.einsum(
        "orm,rm->om", derivative_entering.reshape(samples, sub_dev, width), gain_row_values
    )
    enc_order = derivative_bottleneck[sample_index]
    owned_rows = lax.psum_scatter(enc_order, "freq", scatter_dimension=0, tiled=True)
    grad_enc, grad_dec = encoder_grads(encoder_input, codes_own, owned_rows, decoder_weight)
    grad_enc, grad_dec, grad_out, grad_filter = lax.psum(
        (grad_enc, grad_dec, grad_out, grad_filter), "freq"
    )
    return (grad_enc, grad_dec, grad_out, grad_filter)


def solution(mesh):
    return jax.shard_map(
        local,
        mesh=mesh,
        in_specs=(
            P(("groups", "freq"), None),
            P("groups", "freq", None),
            P("groups"),
            P(),
            P(),
            P("freq", None),
            P(),
            P(),
        ),
        out_specs=(P("groups", None), P("groups", None), P("groups", None), P("groups", None)),
        check_vma=False,
    )
```

profile of v0, /device:TPU:0, one launch (start us, length us, event | category | flops | bytes accessed | tf_op | source)
XLA Modules:
  0.0 264.4 jit_solution(11074158935546057527)
XLA Ops:
  7.2 0.0 all-reduce.5.cloned.1.call-start
  7.3 1.0 fusion.30
  8.3 1.1 negate_convert_fusion
  9.4 0.7 compare_select_fusion.1
  10.1 0.7 scatter_custom_fusion
  10.8 0.8 fusion.54
  11.6 1.1 fusion.8
  12.7 23.2 %all-gather = bf16[16,2,512]{2,1,0:T(2,128)(2,1)S(1)} all-gather(bf16[1,2,512]{2,1,0:T(2,128)(2,1)S(1)} %bitcast.34), channel_id=1, replica_groups=mesh['groups'=2,'freq'=16] {'freq'}, dimensions={0}, use_global_device_ids=true | all-gather | bytes 34816 | tf_op jit(solution)/shard_map/all_gather | solution.py:116
  35.9 0.6 gather_fusion
  36.5 0.2 fusion.55
  36.7 0.2 multiply_convert_fusion
  36.9 0.6 fusion.34
  37.4 0.2 subtract_convert_fusion.1
  37.7 1.0 add_convert_fusion
  38.7 0.3 copy-done.10
  39.0 0.6 fusion.7
  39.6 1.6 fusion.21
  41.2 0.6 convolution_add_fusion.1
  41.8 1.2 fusion.17
  43.1 0.4 add_reduce_fusion
  43.5 0.2 copy-done.11
  43.7 0.6 dynamic-slice
  45.0 2.3 convolution_add_fusion
  47.3 0.3 multiply_reduce_fusion
  47.6 0.6 gather_fusion.1
  48.2 59.2 %all-reduce.1 = (bf16[32,512]{1,0:T(8,128)(2,1)S(1)}, f32[2,256]{1,0:T(2,128)}) all-reduce(f32[32,512]{1,0:T(8,128)S(1)} %gather_fusion.1, f32[2,256]{1,0:T(2,128)S(1)} %pad_maximum_fusion.4), channel_id=2, replica_groups=mesh['groups'=2,'freq'=16] {'freq'}, use_global_device_ids=true, to_apply=%region_1.2.clone | all-reduce | flops 16896 | bytes 102400
  107.4 1.3 fusion.53
  108.7 3.0 %convolution_bitcast_fusion = f32[2048,512]{0,1:T(8,128)} fusion(bf16[2,2048]{1,0:T(2,128)(2,1)S(1)} %copy-done.8, bf16[512,512]{1,0:T(8,128)(2,1)S(1)} %copy-done.1, bf16[2,512]{1,0:T(2,128)(2,1)S(1)} %fusion.8, bf16[32,512]{1,0:T(8,128)(2,1)S(1)} %get-tuple-element.14, u32[]{:T(128)S(6)} %multiply.6), kind=kOutput, calls=%fused_computation.3 | convolution fusion | flops 5248000 | bytes 4730884 | tf_op jit(solution)/shard_map/dot_general | solution.py:92
  111.8 137.2 %all-reduce.5.cloned.1.call-done = (f32[2048,512]{0,1:T(8,128)}, f32[512,512]{1,0:T(8,128)}, f32[512,512]{1,0:T(8,128)}) async-done(((f32[2048,512]{0,1:T(8,128)}, f32[512,512]{1,0:T(8,128)}, f32[512,512]{1,0:T(8,128)}), (f32[2048,512]{0,1:T(8,128)}, f32[512,512]{1,0:T(8,128)}, f32[512,512]{1,0:T(8,128)})) %all-reduce.5.cloned.1.call-update) | async-done | bytes 6291472 | tf_op jit(solution)/shard_map/psum | solution.py:139
  248.9 5.3 %copy.13 = f32[2048,512]{1,0:T(8,128)} copy(f32[2048,512]{0,1:T(8,128)} %get-tuple-element.16) | data formatting | bytes 8388608
  254.3 2.4 copy.25
  256.6 1.0 copy.26
  (30 shorter events, 0.2 us)
Async XLA Ops:
  7.2 4.4 %copy-start = (bf16[2048,512]{1,0:T(8,128)(2,1)S(1)}, bf16[2048,512]{1,0:T(8,128)(2,1)}, u32[]{:S(2)}) copy-start(bf16[2048,512]{1,0:T(8,128)(2,1)} %param.11) | copy-start | bytes 6291460
  7.2 28.7 %copy-start.9 = (bf16[24,512]{1,0:T(8,128)(2,1)S(1)}, bf16[24,512]{1,0:T(8,128)(2,1)}, u32[]{:S(2)}) copy-start(bf16[24,512]{1,0:T(8,128)(2,1)} %param.13) | copy-start | bytes 73732
  7.2 29.3 %copy-start.1 = (bf16[512,512]{1,0:T(8,128)(2,1)S(1)}, bf16[512,512]{1,0:T(8,128)(2,1)}, u32[]{:S(2)}) copy-start(bf16[512,512]{1,0:T(8,128)(2,1)} %param.12) | copy-start | bytes 1572868
  7.2 241.7 %all-reduce.5.cloned.1.call-start = ((), (), s32[]{:S(2)}) async-start(), calls=%async_computation | async-start | bytes 12582912 | tf_op jit(solution)/shard_map/psum | solution.py:139
  8.3 33.6 %copy-start.5 = (bf16[256,256]{1,0:T(8,128)(2,1)}, bf16[256,256]{1,0:T(8,128)(2,1)S(1)}, u32[]{:S(2)}) copy-start(bf16[256,256]{1,0:T(8,128)(2,1)S(1)} %fusion.30) | copy-start | bytes 393220
  9.4 32.4 %copy-start.6 = (bf16[256,256]{1,0:T(8,128)(2,1)}, bf16[256,256]{1,0:T(8,128)(2,1)S(1)}, u32[]{:S(2)}) copy-start(bf16[256,256]{1,0:T(8,128)(2,1)S(1)} %get-tuple-element.31) | copy-start | bytes 393220
  9.4 32.4 %copy-start.7 = (bf16[256,256]{1,0:T(8,128)(2,1)}, bf16[256,256]{1,0:T(8,128)(2,1)S(1)}, u32[]{:S(2)}) copy-start(bf16[256,256]{1,0:T(8,128)(2,1)S(1)} %get-tuple-element.32) | copy-start | bytes 393220
  37.7 1.0 copy-start.4
  37.7 1.3 copy-start.10
  41.8 1.3 copy-start.2
  43.1 0.7 copy-start.11
  47.2 61.5 %copy-start.8 = (bf16[2,2048]{1,0:T(2,128)(2,1)S(1)}, bf16[2,2048]{1,0:T(2,128)(2,1)}, u32[]{:S(2)}) copy-start(bf16[2,2048]{1,0:T(2,128)(2,1)} %param.8) | copy-start | bytes 24580
  254.3 2.4 copy-start.3
Sparse Core Ops, SparseCore 0:
  111.9 136.9 all-reduce.4
where the time goes:
time: 265 us; the launch traced here: 264 us
  waiting for transfers between devices  137 us (52%)
  blocking collectives  82.4 us (31%)
  between operations  14.9 us (6%)
  matrix products  13.4 us (5%)
  local copies, waits for them, and re-layouts  12.5 us (5%)
  other arithmetic  3.97 us (1%)
    psum x1, waiting for transfers between devices, local(): lax.psum((grad_enc, grad_dec, grad_out, grad_filter), 'freq')  137 us
    unnamed x1, blocking collectives  59.2 us
    all_gather x1, blocking collectives, local(): all_codes = lax.all_gather(codes_own, 'freq', axis=0, tiled=True)  23.2 us
    unnamed x29, local copies, waits for them, and re-layouts  9.8 us
  transfers between devices with their start and end apart: 1, of which 1 were waited for; matrix products, arithmetic and copies ran while one was open for 0% of the time, Pallas kernels for 0%

commit v1 on v0

--- a/solution.py
+++ b/solution.py
@@ -3,6 +3,25 @@
 import jax.numpy as jnp
 from jax import lax
 from jax.sharding import PartitionSpec as P
+
+
+def ring_gather(x, axis, dim):
+    size, place, rows = (lax.axis_size(axis), lax.axis_index(axis), x.shape[dim])
+    right = [(i, (i + 1) % size) for i in range(size)]
+    backward = [(i, (i - 1) % size) for i in range(size)]
+    out = jnp.zeros((*x.shape[:dim], size * rows, *x.shape[dim + 1 :]), x.dtype)
+    out = lax.dynamic_update_slice_in_dim(out, x, place * rows, axis=dim)
+    from_left = from_right = x
+    middle = size // 2
+    for lap in range(1, middle + 1):
+        from_left = lax.ppermute(from_left, axis, right)
+        out = lax.dynamic_update_slice_in_dim(out, from_left, (place - lap) % size * rows, axis=dim)
+        if lap < size - middle:
+            from_right = lax.ppermute(from_right, axis, backward)
+            out = lax.dynamic_update_slice_in_dim(
+                out, from_right, (place + lap) % size * rows, axis=dim
+            )
+    return out
 
 
 def rotation_tables(antennas):
@@ -113,7 +132,7 @@
     codes_own = jnp.tanh(
         jnp.dot(encoder_input, encoder_weight, preferred_element_type=jnp.float32)
     ).astype(jnp.bfloat16)
-    all_codes = lax.all_gather(codes_own, "freq", axis=0, tiled=True)
+    all_codes = ring_gather(codes_own, "freq", 0)
     inverse_ids = (
         jnp.zeros((samples,), jnp.int32).at[sample_index].set(jnp.arange(samples, dtype=jnp.int32))
     )

time: 265 us -> 289 us (1.091)
  starting transfers between devices: 0.04 us -> 32 us
  blocking collectives: 82.4 us -> 58.9 us
  waiting for transfers between devices: 137 us -> 155 us
    ppermute x0 -> x15, starting transfers between devices: none -> 32 us  [the longest x7 32 us: ring_gather(): from_right = lax.ppermute(from_right, axis, backward)]
    all_gather x1 -> x0, blocking collectives: 23.2 us -> none  [local(): all_codes = lax.all_gather(codes_own, 'freq', axis=0, tiled=True)]
    ppermute x0 -> x15, waiting for transfers between devices: none -> 17.7 us  [the longest x8 11.4 us: ring_gather(): from_left = lax.ppermute(from_left, axis, right)]
    unnamed x29 -> x26, local copies, waits for them, and re-layouts: 9.8 us -> 10.4 us
  transfers between devices with their start and end apart: 1 -> 16, of which waited for: 1 -> 8; matrix products, arithmetic and copies ran while one was open for 0% -> 1% of each run, Pallas kernels for 0% -> 0%
where the time goes in v1:
time: 289 us
  waiting for transfers between devices  155 us (54%)
  blocking collectives  58.9 us (20%)
  starting transfers between devices  32 us (11%)
  between operations  15.1 us (5%)
  local copies, waits for them, and re-layouts  12.5 us (4%)
  matrix products  11.8 us (4%)
  other arithmetic  3.27 us (1%)
    psum x1, waiting for transfers between devices, local(): lax.psum((grad_enc, grad_dec, grad_out, grad_filter), 'freq')  137 us
    unnamed x1, blocking collectives  58.9 us
    ppermute x7, starting transfers between devices, ring_gather(): from_right = lax.ppermute(from_right, axis, backward)  32 us
    ppermute x8, waiting for transfers between devices, ring_gather(): from_left = lax.ppermute(from_left, axis, right)  11.4 us
    unnamed x26, local copies, waits for them, and re-layouts  10.4 us
    ppermute x7, waiting for transfers between devices, ring_gather(): from_right = lax.ppermute(from_right, axis, backward)  6.36 us
  transfers between devices with their start and end apart: 16, of which 8 were waited for; matrix products, arithmetic and copies ran while one was open for 1% of the time, Pallas kernels for 0%

profile of v1, /device:TPU:0, one launch (start us, length us, event | category | flops | bytes accessed | tf_op | source)
XLA Modules:
  0.0 288.6 jit_solution(1016130971863387611)
XLA Ops:
  7.3 1.5 copy-done
  8.8 1.1 constant_dynamic-update-slice_fusion.15
  9.9 5.5 %collective-permute-start.1 = (bf16[2,512]{1,0:T(2,128)(2,1)S(1)}, bf16[2,512]{1,0:T(2,128)(2,1)S(1)}, u32[]{:S(2)}, u32[]{:S(2)}) collective-permute-start(bf16[2,512]{1,0:T(2,128)(2,1)S(1)} %get-tuple-element.30), channel_id=1, source_target_pairs={{0,15},{1,0},{2,1},{3,2},{4,3},{5,4},{6,5},{7,6},{8,7},{9,8},{10,9... | collective-permute-start | bytes 6152 | tf_op jit(solution)/shard_map/ppermute | solution.py:20
  15.4 1.0 fusion.30
  16.4 1.1 negate_convert_fusion
  17.6 0.7 scatter_custom_fusion
  19.7 4.5 %collective-permute-start.3 = (bf16[2,512]{1,0:T(2,128)(2,1)S(1)}, bf16[2,512]{1,0:T(2,128)(2,1)S(1)}, u32[]{:S(2)}, u32[]{:S(2)}) collective-permute-start(bf16[2,512]{1,0:T(2,128)(2,1)S(1)} %collective-permute-done.1), channel_id=1, source_target_pairs={{0,15},{1,0},{2,1},{3,2},{4,3},{5,4},{6,5},{7,6},{8,7},{9,8},{10,9... | collective-permute-start | bytes 6152 | tf_op jit(solution)/shard_map/ppermute | solution.py:20
  24.2 1.3 collective-permute-done.3
  25.5 4.4 %collective-permute-start.5 = (bf16[2,512]{1,0:T(2,128)(2,1)S(1)}, bf16[2,512]{1,0:T(2,128)(2,1)S(1)}, u32[]{:S(2)}, u32[]{:S(2)}) collective-permute-start(bf16[2,512]{1,0:T(2,128)(2,1)S(1)} %collective-permute-done.3), channel_id=1, source_target_pairs={{0,15},{1,0},{2,1},{3,2},{4,3},{5,4},{6,5},{7,6},{8,7},{9,8},{10,9... | collective-permute-start | bytes 6152 | tf_op jit(solution)/shard_map/ppermute | solution.py:20
  29.9 1.3 collective-permute-done.5
  31.2 4.4 %collective-permute-start.7 = (bf16[2,512]{1,0:T(2,128)(2,1)S(1)}, bf16[2,512]{1,0:T(2,128)(2,1)S(1)}, u32[]{:S(2)}, u32[]{:S(2)}) collective-permute-start(bf16[2,512]{1,0:T(2,128)(2,1)S(1)} %collective-permute-done.5), channel_id=1, source_target_pairs={{0,15},{1,0},{2,1},{3,2},{4,3},{5,4},{6,5},{7,6},{8,7},{9,8},{10,9... | collective-permute-start | bytes 6152 | tf_op jit(solution)/shard_map/ppermute | solution.py:20
  35.6 1.3 collective-permute-done.7
  36.9 4.4 %collective-permute-start.9 = (bf16[2,512]{1,0:T(2,128)(2,1)S(1)}, bf16[2,512]{1,0:T(2,128)(2,1)S(1)}, u32[]{:S(2)}, u32[]{:S(2)}) collective-permute-start(bf16[2,512]{1,0:T(2,128)(2,1)S(1)} %collective-permute-done.7), channel_id=1, source_target_pairs={{0,15},{1,0},{2,1},{3,2},{4,3},{5,4},{6,5},{7,6},{8,7},{9,8},{10,9... | collective-permute-start | bytes 6152 | tf_op jit(solution)/shard_map/ppermute | solution.py:20
  41.4 1.3 collective-permute-done.9
  42.6 4.4 %collective-permute-start.11 = (bf16[2,512]{1,0:T(2,128)(2,1)S(1)}, bf16[2,512]{1,0:T(2,128)(2,1)S(1)}, u32[]{:S(2)}, u32[]{:S(2)}) collective-permute-start(bf16[2,512]{1,0:T(2,128)(2,1)S(1)} %collective-permute-done.9), channel_id=1, source_target_pairs={{0,15},{1,0},{2,1},{3,2},{4,3},{5,4},{6,5},{7,6},{8,7},{9,8},{10,9... | collective-permute-start | bytes 6152 | tf_op jit(solution)/shard_map/ppermute | solution.py:20
  47.1 1.3 collective-permute-done.11
  48.3 4.4 %collective-permute-start.13 = (bf16[2,512]{1,0:T(2,128)(2,1)S(1)}, bf16[2,512]{1,0:T(2,128)(2,1)S(1)}, u32[]{:S(2)}, u32[]{:S(2)}) collective-permute-start(bf16[2,512]{1,0:T(2,128)(2,1)S(1)} %collective-permute-done.11), channel_id=1, source_target_pairs={{0,15},{1,0},{2,1},{3,2},{4,3},{5,4},{6,5},{7,6},{8,7},{9,8},{10,9... | collective-permute-start | bytes 6152 | tf_op jit(solution)/shard_map/ppermute | solution.py:20
  52.8 5.7 %collective-permute-done.12 = bf16[2,512]{1,0:T(2,128)(2,1)S(1)} collective-permute-done((bf16[2,512]{1,0:T(2,128)(2,1)S(1)}, bf16[2,512]{1,0:T(2,128)(2,1)S(1)}, u32[]{:S(2)}, u32[]{:S(2)}) %collective-permute-start.12) | collective-permute-done | bytes 2080 | tf_op jit(solution)/shard_map/ppermute | solution.py:17
  58.5 5.7 %collective-permute-done.14 = bf16[2,512]{1,0:T(2,128)(2,1)S(1)} collective-permute-done((bf16[2,512]{1,0:T(2,128)(2,1)S(1)}, bf16[2,512]{1,0:T(2,128)(2,1)S(1)}, u32[]{:S(2)}, u32[]{:S(2)}) %collective-permute-start.14) | collective-permute-done | bytes 2080 | tf_op jit(solution)/shard_map/ppermute | solution.py:17
  64.2 0.6 gather_fusion
  66.0 1.0 add_convert_fusion
  67.3 0.6 fusion.7
  67.9 1.6 fusion.21
  70.1 1.2 fusion.17
  73.3 58.9 %all-reduce.1 = (bf16[32,512]{1,0:T(8,128)(2,1)S(1)}, f32[2,256]{1,0:T(2,128)}) all-reduce(f32[32,512]{1,0:T(8,128)S(1)} %gather_fusion.1, f32[2,256]{1,0:T(2,128)S(1)} %pad_maximum_fusion.4), channel_id=2, replica_groups=mesh['groups'=2,'freq'=16] {'freq'}, use_global_device_ids=true, to_apply=%region_1.2.clone | all-reduce | flops 16896 | bytes 102400
  132.2 1.3 fusion.53
  133.6 3.0 %convolution_bitcast_fusion = f32[2048,512]{0,1:T(8,128)} fusion(bf16[2,2048]{1,0:T(2,128)(2,1)S(1)} %copy-done.5, bf16[512,512]{1,0:T(8,128)(2,1)S(1)} %copy-done.1, bf16[2,512]{1,0:T(2,128)(2,1)S(1)} %get-tuple-element.30, bf16[32,512]{1,0:T(8,128)(2,1)S(1)} %get-tuple-element.14, u32[]{:T(128)S(6)} %multiply.6), kind=kOutput, calls=%fused_computation.3 | convolution fusion | flops 5248000 | bytes 4730884 | tf_op jit(solution)/shard_map/dot_general | solution.py:111
  136.6 137.2 %all-reduce.5.cloned.1.call-done = (f32[2048,512]{0,1:T(8,128)}, f32[512,512]{1,0:T(8,128)}, f32[512,512]{1,0:T(8,128)}) async-done(((f32[2048,512]{0,1:T(8,128)}, f32[512,512]{1,0:T(8,128)}, f32[512,512]{1,0:T(8,128)}), (f32[2048,512]{0,1:T(8,128)}, f32[512,512]{1,0:T(8,128)}, f32[512,512]{1,0:T(8,128)})) %all-reduce.5.cloned.1.call-update) | async-done | bytes 6291472 | tf_op jit(solution)/shard_map/psum | solution.py:158
  273.8 5.4 %copy.13 = f32[2048,512]{1,0:T(8,128)} copy(f32[2048,512]{0,1:T(8,128)} %get-tuple-element.16) | data formatting | bytes 8388608
  279.2 1.0 copy.41
  280.2 0.6 copy-done.2
  280.8 1.0 copy.42
  (72 shorter events, 5.0 us)
Async XLA Ops:
  7.2 1.6 copy-start
  7.2 10.3 %copy-start.9 = (s32[32]{0:T(128)S(1)}, s32[32]{0:T(128)}, u32[]{:S(2)}) copy-start(s32[32]{0:T(128)} %param.10) | copy-start | bytes 388
  7.2 11.1 %copy-start.7 = (f32[2,256]{1,0:T(2,128)S(1)}, f32[2,256]{1,0:T(2,128)}, u32[]{:S(2)}) copy-start(f32[2,256]{1,0:T(2,128)} %param.14) | copy-start | bytes 6148
  7.2 11.1 %copy-start.6 = (bf16[24,512]{1,0:T(8,128)(2,1)S(1)}, bf16[24,512]{1,0:T(8,128)(2,1)}, u32[]{:S(2)}) copy-start(bf16[24,512]{1,0:T(8,128)(2,1)} %param.13) | copy-start | bytes 73732
  7.2 266.5 %all-reduce.5.cloned.1.call-start = ((), (), s32[]{:S(2)}) async-start(), calls=%async_computation | async-start | bytes 12582912 | tf_op jit(solution)/shard_map/psum | solution.py:158
  8.8 9.7 %copy-start.10 = (u32[32]{0:T(128)S(1)}, u32[32]{0:T(128)}, u32[]{:S(2)}) copy-start(u32[32]{0:T(128)} %constant.154) | copy-start | bytes 388
  8.8 56.0 %copy-start.1 = (bf16[512,512]{1,0:T(8,128)(2,1)S(1)}, bf16[512,512]{1,0:T(8,128)(2,1)}, u32[]{:S(2)}) copy-start(bf16[512,512]{1,0:T(8,128)(2,1)} %param.12) | copy-start | bytes 1572868
  9.9 9.8 %collective-permute-start.1 = (bf16[2,512]{1,0:T(2,128)(2,1)S(1)}, bf16[2,512]{1,0:T(2,128)(2,1)S(1)}, u32[]{:S(2)}, u32[]{:S(2)}) collective-permute-start(bf16[2,512]{1,0:T(2,128)(2,1)S(1)} %get-tuple-element.30), channel_id=1, source_target_pairs={{0,15},{1,0},{2,1},{3,2},{4,3},{5,4},{6,5},{7,6},{8,7},{9,8},{10,9... | collective-permute-start | bytes 6152 | tf_op jit(solution)/shard_map/ppermute | solution.py:20
  15.4 8.8 %collective-permute-start = (bf16[2,512]{1,0:T(2,128)(2,1)S(1)}, bf16[2,512]{1,0:T(2,128)(2,1)S(1)}, u32[]{:S(2)}, u32[]{:S(2)}) collective-permute-start(bf16[2,512]{1,0:T(2,128)(2,1)S(1)} %get-tuple-element.30), channel_id=1, source_target_pairs={{0,1},{1,2},{2,3},{3,4},{4,5},{5,6},{6,7},{7,8},{8,9},{9,10},{10,1... | collective-permute-start | bytes 6152 | tf_op jit(solution)/shard_map/ppermute | solution.py:17
  19.7 5.8 %collective-permute-start.3 = (bf16[2,512]{1,0:T(2,128)(2,1)S(1)}, bf16[2,512]{1,0:T(2,128)(2,1)S(1)}, u32[]{:S(2)}, u32[]{:S(2)}) collective-permute-start(bf16[2,512]{1,0:T(2,128)(2,1)S(1)} %collective-permute-done.1), channel_id=1, source_target_pairs={{0,15},{1,0},{2,1},{3,2},{4,3},{5,4},{6,5},{7,6},{8,7},{9,8},{10,9... | collective-permute-start | bytes 6152 | tf_op jit(solution)/shard_map/ppermute | solution.py:20
  24.2 5.7 %collective-permute-start.2 = (bf16[2,512]{1,0:T(2,128)(2,1)S(1)}, bf16[2,512]{1,0:T(2,128)(2,1)S(1)}, u32[]{:S(2)}, u32[]{:S(2)}) collective-permute-start(bf16[2,512]{1,0:T(2,128)(2,1)S(1)} %collective-permute-done), channel_id=1, source_target_pairs={{0,1},{1,2},{2,3},{3,4},{4,5},{5,6},{6,7},{7,8},{8,9},{9,10},{10,1... | collective-permute-start | bytes 6152 | tf_op jit(solution)/shard_map/ppermute | solution.py:17
  25.5 5.7 %collective-permute-start.5 = (bf16[2,512]{1,0:T(2,128)(2,1)S(1)}, bf16[2,512]{1,0:T(2,128)(2,1)S(1)}, u32[]{:S(2)}, u32[]{:S(2)}) collective-permute-start(bf16[2,512]{1,0:T(2,128)(2,1)S(1)} %collective-permute-done.3), channel_id=1, source_target_pairs={{0,15},{1,0},{2,1},{3,2},{4,3},{5,4},{6,5},{7,6},{8,7},{9,8},{10,9... | collective-permute-start | bytes 6152 | tf_op jit(solution)/shard_map/ppermute | solution.py:20
  29.9 5.7 %collective-permute-start.4 = (bf16[2,512]{1,0:T(2,128)(2,1)S(1)}, bf16[2,512]{1,0:T(2,128)(2,1)S(1)}, u32[]{:S(2)}, u32[]{:S(2)}) collective-permute-start(bf16[2,512]{1,0:T(2,128)(2,1)S(1)} %collective-permute-done.2), channel_id=1, source_target_pairs={{0,1},{1,2},{2,3},{3,4},{4,5},{5,6},{6,7},{7,8},{8,9},{9,10},{10,1... | collective-permute-start | bytes 6152 | tf_op jit(solution)/shard_map/ppermute | solution.py:17
  31.2 5.7 %collective-permute-start.7 = (bf16[2,512]{1,0:T(2,128)(2,1)S(1)}, bf16[2,512]{1,0:T(2,128)(2,1)S(1)}, u32[]{:S(2)}, u32[]{:S(2)}) collective-permute-start(bf16[2,512]{1,0:T(2,128)(2,1)S(1)} %collective-permute-done.5), channel_id=1, source_target_pairs={{0,15},{1,0},{2,1},{3,2},{4,3},{5,4},{6,5},{7,6},{8,7},{9,8},{10,9... | collective-permute-start | bytes 6152 | tf_op jit(solution)/shard_map/ppermute | solution.py:20
  35.6 5.7 %collective-permute-start.6 = (bf16[2,512]{1,0:T(2,128)(2,1)S(1)}, bf16[2,512]{1,0:T(2,128)(2,1)S(1)}, u32[]{:S(2)}, u32[]{:S(2)}) collective-permute-start(bf16[2,512]{1,0:T(2,128)(2,1)S(1)} %collective-permute-done.4), channel_id=1, source_target_pairs={{0,1},{1,2},{2,3},{3,4},{4,5},{5,6},{6,7},{7,8},{8,9},{9,10},{10,1... | collective-permute-start | bytes 6152 | tf_op jit(solution)/shard_map/ppermute | solution.py:17
  36.9 5.7 %collective-permute-start.9 = (bf16[2,512]{1,0:T(2,128)(2,1)S(1)}, bf16[2,512]{1,0:T(2,128)(2,1)S(1)}, u32[]{:S(2)}, u32[]{:S(2)}) collective-permute-start(bf16[2,512]{1,0:T(2,128)(2,1)S(1)} %collective-permute-done.7), channel_id=1, source_target_pairs={{0,15},{1,0},{2,1},{3,2},{4,3},{5,4},{6,5},{7,6},{8,7},{9,8},{10,9... | collective-permute-start | bytes 6152 | tf_op jit(solution)/shard_map/ppermute | solution.py:20
  41.3 5.7 %collective-permute-start.8 = (bf16[2,512]{1,0:T(2,128)(2,1)S(1)}, bf16[2,512]{1,0:T(2,128)(2,1)S(1)}, u32[]{:S(2)}, u32[]{:S(2)}) collective-permute-start(bf16[2,512]{1,0:T(2,128)(2,1)S(1)} %collective-permute-done.6), channel_id=1, source_target_pairs={{0,1},{1,2},{2,3},{3,4},{4,5},{5,6},{6,7},{7,8},{8,9},{9,10},{10,1... | collective-permute-start | bytes 6152 | tf_op jit(solution)/shard_map/ppermute | solution.py:17
  42.6 5.7 %collective-permute-start.11 = (bf16[2,512]{1,0:T(2,128)(2,1)S(1)}, bf16[2,512]{1,0:T(2,128)(2,1)S(1)}, u32[]{:S(2)}, u32[]{:S(2)}) collective-permute-start(bf16[2,512]{1,0:T(2,128)(2,1)S(1)} %collective-permute-done.9), channel_id=1, source_target_pairs={{0,15},{1,0},{2,1},{3,2},{4,3},{5,4},{6,5},{7,6},{8,7},{9,8},{10,9... | collective-permute-start | bytes 6152 | tf_op jit(solution)/shard_map/ppermute | solution.py:20
  47.0 5.7 %collective-permute-start.10 = (bf16[2,512]{1,0:T(2,128)(2,1)S(1)}, bf16[2,512]{1,0:T(2,128)(2,1)S(1)}, u32[]{:S(2)}, u32[]{:S(2)}) collective-permute-start(bf16[2,512]{1,0:T(2,128)(2,1)S(1)} %collective-permute-done.8), channel_id=1, source_target_pairs={{0,1},{1,2},{2,3},{3,4},{4,5},{5,6},{6,7},{7,8},{8,9},{9,10},{10,1... | collective-permute-start | bytes 6152 | tf_op jit(solution)/shard_map/ppermute | solution.py:17
  48.3 10.1 %collective-permute-start.13 = (bf16[2,512]{1,0:T(2,128)(2,1)S(1)}, bf16[2,512]{1,0:T(2,128)(2,1)S(1)}, u32[]{:S(2)}, u32[]{:S(2)}) collective-permute-start(bf16[2,512]{1,0:T(2,128)(2,1)S(1)} %collective-permute-done.11), channel_id=1, source_target_pairs={{0,15},{1,0},{2,1},{3,2},{4,3},{5,4},{6,5},{7,6},{8,7},{9,8},{10,9... | collective-permute-start | bytes 6152 | tf_op jit(solution)/shard_map/ppermute | solution.py:20
  52.7 5.7 %collective-permute-start.12 = (bf16[2,512]{1,0:T(2,128)(2,1)S(1)}, bf16[2,512]{1,0:T(2,128)(2,1)S(1)}, u32[]{:S(2)}, u32[]{:S(2)}) collective-permute-start(bf16[2,512]{1,0:T(2,128)(2,1)S(1)} %collective-permute-done.10), channel_id=1, source_target_pairs={{0,1},{1,2},{2,3},{3,4},{4,5},{5,6},{6,7},{7,8},{8,9},{9,10},{10,1... | collective-permute-start | bytes 6152 | tf_op jit(solution)/shard_map/ppermute | solution.py:17
  58.4 5.7 %collective-permute-start.14 = (bf16[2,512]{1,0:T(2,128)(2,1)S(1)}, bf16[2,512]{1,0:T(2,128)(2,1)S(1)}, u32[]{:S(2)}, u32[]{:S(2)}) collective-permute-start(bf16[2,512]{1,0:T(2,128)(2,1)S(1)} %collective-permute-done.12), channel_id=1, source_target_pairs={{0,1},{1,2},{2,3},{3,4},{4,5},{5,6},{6,7},{7,8},{8,9},{9,10},{10,1... | collective-permute-start | bytes 6152 | tf_op jit(solution)/shard_map/ppermute | solution.py:17
  66.0 1.0 copy-start.4
  66.0 1.3 copy-start.8
  72.4 61.2 %copy-start.5 = (bf16[2,2048]{1,0:T(2,128)(2,1)S(1)}, bf16[2,2048]{1,0:T(2,128)(2,1)}, u32[]{:S(2)}) copy-start(bf16[2,2048]{1,0:T(2,128)(2,1)} %param.8) | copy-start | bytes 24580
  273.8 5.4 %copy-start.3 = (f32[512,512]{1,0:T(8,128)S(1)}, f32[512,512]{1,0:T(8,128)}, u32[]{:S(2)}) copy-start(f32[512,512]{1,0:T(8,128)} %get-tuple-element.36) | copy-start | bytes 3145732
  279.2 1.6 copy-start.2
Sparse Core Ops, SparseCore 0:
  136.7 136.9 all-reduce.4
